TPU v7x, 512 devices: a whole 4x4x16 slice. The times are simulated.
512 devices in a mesh: ctx: 64 (over x_hi, z, core), mp: 8 (over x_lo, y).
Axes of the slice: x: 4 (x_hi: 2, x_lo: 2; x = x_hi * 2 + x_lo), y: 4, z: 16, core: 2. Of those that a mesh axis runs over, the one named last changes fastest.
Arguments:
- queries: bfloat16 [4096, 8192], P('ctx', 'mp'), may hold values from -8 to 8
- keys: bfloat16 [4096, 1024], P('ctx', 'mp'), may hold values from -8 to 8
- values: bfloat16 [4096, 1024], P('ctx', 'mp'), may hold values from -6 to 6
- positions: int32 [4096], P('ctx'), may hold values from 0 to 4095, as said below
- x_normed: bfloat16 [4096, 8192], P('ctx', 'mp'), may hold values from -6 to 6
- w_gate: bfloat16 [8192, 16384], P('mp', 'ctx'), may hold values from -0.0625 to 0.0625
- w_up: bfloat16 [8192, 16384], P('mp', 'ctx'), may hold values from -0.0625 to 0.0625
Outputs:
- attended: bfloat16 [4096, 8192], P('ctx', 'mp')
- mlp_hidden: bfloat16 [4096, 16384], P('mp', 'ctx')
Inputs may be any that keep to these rules, and one draw needn't show every extreme that they name: `positions`: each position of 0 to 4095 appears exactly once.
All inputs are finite; a program needn't handle non-finite values.
Results may differ from a plain program's by a relative error of at most 0.02.
Values may be sent and summed in bfloat16 or wider, within the bound.
No kernel may reach another device: no remote copies, remote signals or barrier semaphores. Data moves between devices by JAX's collectives and lax.ppermute only.
A program may use at most 64 MiB of HBM per device.

v0:
```python
import jax
import jax.numpy as jnp
from jax import lax
from jax.sharding import PartitionSpec as P

HEAD = 128


def per_device(queries, keys, values, positions, x_normed, w_gate, w_up):
    tok_rows = queries.shape[0]
    local_heads = queries.shape[1] // HEAD
    local_kv = keys.shape[1] // HEAD
    group = local_heads // local_kv
    scale = HEAD ** (-0.5)
    query_four = queries.reshape(tok_rows, local_kv, group, HEAD)
    top_run = jnp.full((local_kv, group, tok_rows), -1e30, jnp.float32)
    k_piece = lax.all_gather(keys, "ctx", axis=0, tiled=True)
    v_piece = lax.all_gather(values, "ctx", axis=0, tiled=True)
    k_pos = lax.all_gather(positions, "ctx", axis=0, tiled=True)
    count = k_piece.shape[0]
    k_three = k_piece.reshape(count, local_kv, HEAD)
    v_three = v_piece.reshape(count, local_kv, HEAD)
    scores = (
        jnp.einsum("tgjd,sgd->gjts", query_four, k_three, preferred_element_type=jnp.float32)
        * scale
    )
    visible = k_pos[None, :] <= positions[:, None]
    piece_top = jnp.max(jnp.where(visible, scores, jnp.float32(-1e30)), axis=-1)
    top_new = jnp.maximum(top_run, piece_top)
    weights = jnp.where(visible, jnp.exp(scores - top_new[..., None]), jnp.float32(0.0))
    total_new = jnp.sum(weights, axis=-1)
    mixed = jnp.einsum(
        "gjts,sgd->gjtd", weights.astype(jnp.bfloat16), v_three, preferred_element_type=jnp.float32
    )
    final_state = (top_new, total_new, mixed)
    top_run, total_run, accum = final_state
    normed = accum / total_run[..., None]
    attended = (
        jnp.transpose(normed, (2, 0, 1, 3))
        .reshape(tok_rows, local_heads * HEAD)
        .astype(jnp.bfloat16)
    )
    hidden_cols = w_gate.shape[1]
    both_weights = jnp.concatenate((w_gate, w_up), axis=1)
    block_terms = jnp.dot(
        lax.all_gather(x_normed, "ctx", axis=0, tiled=True),
        both_weights,
        preferred_element_type=jnp.float32,
    ).astype(jnp.bfloat16)
    summed = lax.psum_scatter(
        block_terms.astype(jnp.float32).astype(jnp.bfloat16), "mp", scatter_dimension=0, tiled=True
    ).astype(jnp.float32)
    gate = summed[:, :hidden_cols]
    up = summed[:, hidden_cols:]
    mlp_hidden = (jax.nn.silu(gate) * up).astype(jnp.bfloat16)
    return (attended, mlp_hidden)


def solution(mesh):
    return jax.shard_map(
        per_device,
        mesh=mesh,
        in_specs=(
            P("ctx", "mp"),
            P("ctx", "mp"),
            P("ctx", "mp"),
            P("ctx"),
            P("ctx", "mp"),
            P("mp", "ctx"),
            P("mp", "ctx"),
        ),
        out_specs=(P("ctx", "mp"), P("mp", "ctx")),
        check_vma=False,
    )
```

profile of v0, /device:TPU:1, one launch (start us, length us, event | category | flops | bytes accessed | tf_op | source)
XLA Modules:
  0.0 528.0 jit_solution(817598872555930921)
XLA Ops:
  7.2 0.0 all-gather.8.cloned.1.call-start
  7.2 0.7 all-gather.8.cloned.1.call-update
  7.9 0.0 all-gather.4.cloned.1.call-start
  8.0 0.7 all-gather.4.cloned.1.call-update
  8.7 0.0 all-gather.6.cloned.1.call-start
  8.7 0.7 all-gather.6.cloned.1.call-update
  9.4 0.0 reduce-scatter.2.cloned.1.call-start
  9.5 172.6 %all-gather.8.cloned.1.call-done = bf16[4096,1024]{1,0:T(8,128)(2,1)} async-done(((bf16[64,1024]{1,0:T(8,128)(2,1)}), bf16[4096,1024]{1,0:T(8,128)(2,1)}) %all-gather.8.cloned.1.call-update) | async-done | bytes 8388624 | tf_op jit(solution)/shard_map/all_gather | solution.py:46
  182.1 10.2 %fusion.5 = bf16[4096,512]{0,1:T(8,128)(2,1)} fusion(bf16[4096,1024]{1,0:T(8,128)(2,1)} %all-gather.8.cloned.1.call-done, bf16[1024,256]{1,0:T(8,128)(2,1)} %param.13, bf16[1024,256]{1,0:T(8,128)(2,1)} %param.12), kind=kOutput, calls=%fused_computation.8 | convolution fusion | flops 4299161600 | bytes 13631488 | tf_op jit(solution)/shard_map/dot_general | solution.py:45
  192.3 1.3 dynamic-slice
  194.3 0.3 dynamic-update-slice
  194.5 251.6 %all-reduce = s32[4096]{0:T(1024)S(1)} all-reduce(s32[4096]{0:T(1024)S(1)} %dynamic-update-slice), channel_id=1, replica_groups=mesh['ctx'=64,'mp'=8] {'ctx'}, use_global_device_ids=true, to_apply=%add | all-reduce | flops 4096 | bytes 32768
  446.1 0.2 broadcast_compare_fusion
  446.4 2.9 fusion
  449.3 3.2 copy-done.1
  452.5 2.4 fusion.3
  454.9 5.6 %all-gather.6.cloned.1.call-done = bf16[4096,128]{1,0:T(8,128)(2,1)} async-done(((bf16[64,128]{1,0:T(8,128)(2,1)}), bf16[4096,128]{1,0:T(8,128)(2,1)}) %all-gather.6.cloned.1.call-update) | async-done | bytes 1048592 | tf_op jit(solution)/shard_map/all_gather | solution.py:18
  460.6 5.2 fusion.16
  465.7 0.1 copy.12
  465.8 0.7 copy.23
  466.5 52.7 %reduce-scatter.2.cloned.1.call-done = bf16[512,512]{0,1:T(8,128)(2,1)} async-done(((bf16[4096,512]{0,1:T(8,128)(2,1)}), bf16[512,512]{0,1:T(8,128)(2,1)}) %reduce-scatter.2.cloned.1.call-update) | async-done | bytes 524304 | tf_op jit(solution)/shard_map/reduce_scatter | solution.py:50
  519.3 1.2 convert_element_type.36
  520.4 0.2 fusion.25
  520.6 0.8 copy.13
  (9 shorter events, 0.1 us)
Async XLA Ops:
  7.2 439.2 %copy-start = (bf16[64,1024]{1,0:T(8,128)(2,1)S(1)}, bf16[64,1024]{1,0:T(8,128)(2,1)}, u32[]{:S(2)}) copy-start(bf16[64,1024]{1,0:T(8,128)(2,1)} %param.7) | copy-start | bytes 393220
  7.2 174.9 %all-gather.8.cloned.1.call-start = ((), (), s32[]{:S(2)}) async-start(), calls=%async_computation.3 | async-start | bytes 8519680 | tf_op jit(solution)/shard_map/all_gather | solution.py:46
  7.9 438.4 %all-gather.4.cloned.1.call-start = ((), (), s32[]{:S(2)}) async-start(), calls=%async_computation.1 | async-start | bytes 1064960 | tf_op jit(solution)/shard_map/all_gather | solution.py:17
  8.7 451.9 %all-gather.6.cloned.1.call-start = ((), (), s32[]{:S(2)}) async-start(), calls=%async_computation.2 | async-start | bytes 1064960 | tf_op jit(solution)/shard_map/all_gather | solution.py:18
  9.4 184.9 %copy-start.2 = (s32[64]{0:T(128)S(1)}, s32[64]{0:T(128)}, u32[]{:S(2)}) copy-start(s32[64]{0:T(128)} %param.10) | copy-start | bytes 772
  9.4 509.9 %reduce-scatter.2.cloned.1.call-start = ((), (), s32[]{:S(2)}) async-start(), calls=%async_computation.4 | async-start | bytes 4718592 | tf_op jit(solution)/shard_map/reduce_scatter | solution.py:50
  449.3 3.2 copy-start.1
Sparse Core Ops, SparseCore 0:
  11.3 170.7 all-gather.7
  185.3 135.2 all-gather.3
  323.9 136.6 all-gather.5
  463.3 55.9 reduce-scatter.1
where the time goes:
time: 528 us
  blocking collectives  252 us (48%)
  waiting for transfers between devices  233 us (44%)
  matrix products  18.3 us (3%)
  between operations  14.5 us (3%)
  local copies, waits for them, and re-layouts  6.38 us (1%)
    unnamed x1, blocking collectives  252 us
    all_gather x1, waiting for transfers between devices, per_device(): lax.all_gather(x_normed, 'ctx', axis=0, tiled=True)  173 us
    reduce_scatter x1, waiting for transfers between devices, per_device(): lax.psum_scatter(block_terms.astype(jnp.float32).astype(jnp.bfloat16), 'm...  52.7 us
  transfers between devices with their start and end apart: 4, of which 3 were waited for; matrix products, arithmetic and copies ran while one was open for 4% of the time, Pallas kernels for 0%

commit v1 on v0

--- a/solution.py
+++ b/solution.py
@@ -14,9 +14,19 @@
     scale = HEAD ** (-0.5)
     query_four = queries.reshape(tok_rows, local_kv, group, HEAD)
     top_run = jnp.full((local_kv, group, tok_rows), -1e30, jnp.float32)
-    k_piece = lax.all_gather(keys, "ctx", axis=0, tiled=True)
-    v_piece = lax.all_gather(values, "ctx", axis=0, tiled=True)
-    k_pos = lax.all_gather(positions, "ctx", axis=0, tiled=True)
+    pos_hi = positions // 64
+    pos_lo = positions - pos_hi * 64
+    pos_cols = jnp.zeros((tok_rows, HEAD), jnp.bfloat16)
+    pos_cols = pos_cols.at[:, 0].set(pos_hi.astype(jnp.bfloat16))
+    pos_cols = pos_cols.at[:, 1].set(pos_lo.astype(jnp.bfloat16))
+    kv_pack = jnp.concatenate((keys, values, pos_cols), axis=1)
+    kv_all = lax.all_gather(kv_pack, "ctx", axis=0, tiled=True)
+    kv_width = keys.shape[1]
+    k_piece = kv_all[:, :kv_width]
+    v_piece = kv_all[:, kv_width : 2 * kv_width]
+    pos_back = kv_all[:, 2 * kv_width :].astype(jnp.float32)
+    k_pos = pos_back[:, 0] * 64.0 + pos_back[:, 1]
+    q_pos = positions.astype(jnp.float32)
     count = k_piece.shape[0]
     k_three = k_piece.reshape(count, local_kv, HEAD)
     v_three = v_piece.reshape(count, local_kv, HEAD)
@@ -24,7 +34,7 @@
         jnp.einsum("tgjd,sgd->gjts", query_four, k_three, preferred_element_type=jnp.float32)
         * scale
     )
-    visible = k_pos[None, :] <= positions[:, None]
+    visible = k_pos[None, :] <= q_pos[:, None]
     piece_top = jnp.max(jnp.where(visible, scores, jnp.float32(-1e30)), axis=-1)
     top_new = jnp.maximum(top_run, piece_top)
     weights = jnp.where(visible, jnp.exp(scores - top_new[..., None]), jnp.float32(0.0))

time: 528 us -> 394 us (0.75)
  blocking collectives: 252 us -> 0 us
  waiting for transfers between devices: 233 us -> 351 us
  other arithmetic: 3.96 us -> 11.1 us
    unnamed x1 -> x0, blocking collectives: 252 us -> none
    all_gather x2 -> x1, waiting for transfers between devices: 5.66 us -> 135 us  [per_device(): kv_all = lax.all_gather(kv_pack, 'ctx', axis=0, tiled=True)]
    reduce_scatter x1, waiting for transfers between devices: 52.7 us -> 46.1 us  [per_device(): lax.psum_scatter(block_terms.astype(jnp.float32).astype(jnp.bfloat16), 'm...]
  transfers between devices with their start and end apart: 4 -> 3, of which waited for: 3 -> 3; matrix products, arithmetic and copies ran while one was open for 4% -> 7% of each run, Pallas kernels for 0% -> 0%
where the time goes in v1:
time: 394 us
  waiting for transfers between devices  351 us (89%)
  matrix products  15.9 us (4%)
  between operations  13.9 us (4%)
  other arithmetic  11.1 us (3%)
    all_gather x1, waiting for transfers between devices, per_device(): lax.all_gather(x_normed, 'ctx', axis=0, tiled=True)  169 us
    all_gather x1, waiting for transfers between devices, per_device(): kv_all = lax.all_gather(kv_pack, 'ctx', axis=0, tiled=True)  135 us
    reduce_scatter x1, waiting for transfers between devices, per_device(): lax.psum_scatter(block_terms.astype(jnp.float32).astype(jnp.bfloat16), 'm...  46.1 us
    dot_general x1, matrix products, per_device(): jnp.dot(lax.all_gather(x_normed, 'ctx', axis=0, tiled=True), both_weights...  10.3 us
  transfers between devices with their start and end apart: 3, of which 3 were waited for; matrix products, arithmetic and copies ran while one was open for 7% of the time, Pallas kernels for 0%

profile of v1, /device:TPU:1, one launch (start us, length us, event | category | flops | bytes accessed | tf_op | source)
XLA Modules:
  0.0 393.5 jit_solution(9480754632313877885)
XLA Ops:
  7.2 0.7 all-gather.5.cloned.1.call-update
  8.0 0.6 compare_reduce_fusion.1
  8.6 0.6 compare_reduce_fusion
  9.2 1.3 fusion.28
  10.6 0.7 fusion.27
  11.2 0.1 copy.13
  11.3 0.1 copy.14
  11.4 0.1 scatter.9
  11.6 1.4 pad_maximum_fusion
  13.0 168.9 %all-gather.5.cloned.1.call-done = bf16[4096,1024]{1,0:T(8,128)(2,1)} async-done(((bf16[64,1024]{1,0:T(8,128)(2,1)}), bf16[4096,1024]{1,0:T(8,128)(2,1)}) %all-gather.5.cloned.1.call-update) | async-done | bytes 8388624 | tf_op jit(solution)/shard_map/all_gather | solution.py:56
  182.0 10.3 %fusion.5 = bf16[4096,512]{0,1:T(8,128)(2,1)} fusion(bf16[4096,1024]{1,0:T(8,128)(2,1)} %all-gather.5.cloned.1.call-done, bf16[1024,256]{1,0:T(8,128)(2,1)} %param.17, bf16[1024,256]{1,0:T(8,128)(2,1)} %param.16), kind=kOutput, calls=%fused_computation.8 | convolution fusion | flops 4299161600 | bytes 13631488 | tf_op jit(solution)/shard_map/dot_general | solution.py:55
  192.3 134.9 %all-gather.3.cloned.1.call-done = bf16[4096,384]{1,0:T(8,128)(2,1)} async-done(((bf16[64,384]{1,0:T(8,128)(2,1)}), bf16[4096,384]{1,0:T(8,128)(2,1)}) %all-gather.3.cloned.1.call-update) | async-done | bytes 3145744 | tf_op jit(solution)/shard_map/all_gather | solution.py:23
  327.2 1.4 slice_convert_fusion
  328.6 1.2 fusion.10
  329.7 0.2 broadcast_compare_fusion
  330.0 2.9 fusion
  332.9 2.4 fusion.3
  335.3 2.8 fusion.17
  338.0 0.1 copy.16
  338.1 0.7 copy.27
  338.8 46.1 %reduce-scatter.2.cloned.1.call-done = bf16[512,512]{0,1:T(8,128)(2,1)} async-done(((bf16[4096,512]{0,1:T(8,128)(2,1)}), bf16[512,512]{0,1:T(8,128)(2,1)}) %reduce-scatter.2.cloned.1.call-update) | async-done | bytes 524304 | tf_op jit(solution)/shard_map/reduce_scatter | solution.py:60
  384.8 1.2 convert_element_type.52
  386.0 0.2 fusion.24
  386.2 0.8 copy.17
  (12 shorter events, 0.2 us)
Async XLA Ops:
  7.2 322.8 %copy-start = (bf16[64,1024]{1,0:T(8,128)(2,1)S(1)}, bf16[64,1024]{1,0:T(8,128)(2,1)}, u32[]{:S(2)}) copy-start(bf16[64,1024]{1,0:T(8,128)(2,1)} %param.11) | copy-start | bytes 393220
  7.2 174.8 %all-gather.5.cloned.1.call-start = ((), (), s32[]{:S(2)}) async-start(), calls=%async_computation.2 | async-start | bytes 8519680 | tf_op jit(solution)/shard_map/all_gather | solution.py:56
  7.9 319.3 %all-gather.3.cloned.1.call-start = ((), (), s32[]{:S(2)}) async-start(), calls=%async_computation.1 | async-start | bytes 3194880 | tf_op jit(solution)/shard_map/all_gather | solution.py:23
  13.0 179.3 %copy-start.1 = (s32[64]{0:T(128)S(1)}, s32[64]{0:T(128)}, u32[]{:S(2)}) copy-start(s32[64]{0:T(128)} %param.14) | copy-start | bytes 772
  13.0 371.8 %reduce-scatter.2.cloned.1.call-start = ((), (), s32[]{:S(2)}) async-start(), calls=%async_computation.3 | async-start | bytes 4718592 | tf_op jit(solution)/shard_map/reduce_scatter | solution.py:60
Sparse Core Ops, SparseCore 0:
  11.3 170.6 all-gather.4
  185.8 141.3 all-gather.2
  330.0 54.7 reduce-scatter.1

commit v2 on v1

--- a/solution.py
+++ b/solution.py
@@ -1,9 +1,10 @@
 import jax
 import jax.numpy as jnp
 from jax import lax
-from jax.sharding import PartitionSpec as P
+from jax.sharding import Mesh, PartitionSpec as P
 
 HEAD = 128
+CTX = ("xh", "zz", "cc")
 
 
 def per_device(queries, keys, values, positions, x_normed, w_gate, w_up):
@@ -20,7 +21,7 @@
     pos_cols = pos_cols.at[:, 0].set(pos_hi.astype(jnp.bfloat16))
     pos_cols = pos_cols.at[:, 1].set(pos_lo.astype(jnp.bfloat16))
     kv_pack = jnp.concatenate((keys, values, pos_cols), axis=1)
-    kv_all = lax.all_gather(kv_pack, "ctx", axis=0, tiled=True)
+    kv_all = lax.all_gather(kv_pack, CTX, axis=0, tiled=True)
     kv_width = keys.shape[1]
     k_piece = kv_all[:, :kv_width]
     v_piece = kv_all[:, kv_width : 2 * kv_width]
@@ -52,33 +53,53 @@
     )
     hidden_cols = w_gate.shape[1]
     both_weights = jnp.concatenate((w_gate, w_up), axis=1)
+    pair_weights = lax.all_gather(both_weights, "cc", axis=1, tiled=True)
+    x_half = lax.all_gather(x_normed, ("xh", "zz"), axis=0, tiled=True)
     block_terms = jnp.dot(
-        lax.all_gather(x_normed, "ctx", axis=0, tiled=True),
-        both_weights,
-        preferred_element_type=jnp.float32,
+        x_half, pair_weights, preferred_element_type=jnp.float32
     ).astype(jnp.bfloat16)
     summed = lax.psum_scatter(
-        block_terms.astype(jnp.float32).astype(jnp.bfloat16), "mp", scatter_dimension=0, tiled=True
+        block_terms, "mp", scatter_dimension=0, tiled=True
     ).astype(jnp.float32)
-    gate = summed[:, :hidden_cols]
-    up = summed[:, hidden_cols:]
-    mlp_hidden = (jax.nn.silu(gate) * up).astype(jnp.bfloat16)
+    width = 2 * hidden_cols
+    per_core = []
+    for owner in range(2):
+        gate = summed[:, owner * width : owner * width + hidden_cols]
+        up = summed[:, owner * width + hidden_cols : (owner + 1) * width]
+        per_core.append((jax.nn.silu(gate) * up).astype(jnp.bfloat16))
+    stacked = jnp.stack(per_core)
+    core = lax.axis_index("cc")
+    mine = stacked[core]
+    other = stacked[1 - core]
+    got = lax.ppermute(other, "cc", [(0, 1), (1, 0)])
+    both = jnp.stack((mine, got))
+    parity0 = both[core]
+    parity1 = both[1 - core]
+    rows = parity0.shape[0]
+    chunk = tok_rows
+    mlp_hidden = jnp.stack(
+        (parity0.reshape(rows // chunk, chunk, hidden_cols), parity1.reshape(rows // chunk, chunk, hidden_cols)),
+        axis=1,
+    ).reshape(2 * rows, hidden_cols)
     return (attended, mlp_hidden)
 
 
 def solution(mesh):
+    n_ctx = mesh.shape["ctx"]
+    n_mp = mesh.shape["mp"]
+    fine = Mesh(mesh.devices.reshape(2, n_ctx // 4, 2, n_mp), ("xh", "zz", "cc", "mp"))
     return jax.shard_map(
         per_device,
-        mesh=mesh,
+        mesh=fine,
         in_specs=(
-            P("ctx", "mp"),
-            P("ctx", "mp"),
-            P("ctx", "mp"),
-            P("ctx"),
-            P("ctx", "mp"),
-            P("mp", "ctx"),
-            P("mp", "ctx"),
+            P(CTX, "mp"),
+            P(CTX, "mp"),
+            P(CTX, "mp"),
+            P(CTX),
+            P(CTX, "mp"),
+            P("mp", CTX),
+            P("mp", CTX),
         ),
-        out_specs=(P("ctx", "mp"), P("mp", "ctx")),
+        out_specs=(P(CTX, "mp"), P("mp", CTX)),
         check_vma=False,
     )

time: 394 us -> 426 us (1.081)
  waiting for transfers between devices: 351 us -> 373 us
    all_gather x2 -> x3, waiting for transfers between devices: 304 us -> 325 us  [the longest x1 157 us: per_device(): x_half = lax.all_gather(x_normed, ('xh', 'zz'), axis=0, tiled=True)]
  transfers between devices with their start and end apart: 3 -> 5, of which waited for: 3 -> 4; matrix products, arithmetic and copies ran while one was open for 7% -> 6% of each run, Pallas kernels for 0% -> 0%
where the time goes in v2:
time: 426 us
  waiting for transfers between devices  373 us (88%)
  matrix products  15.9 us (4%)
  between operations  13.9 us (3%)
  other arithmetic  13.8 us (3%)
  local copies, waits for them, and re-layouts  5.9 us (1%)
    all_gather x1, waiting for transfers between devices, per_device(): x_half = lax.all_gather(x_normed, ('xh', 'zz'), axis=0, tiled=True)  157 us
    all_gather x1, waiting for transfers between devices, per_device(): kv_all = lax.all_gather(kv_pack, CTX, axis=0, tiled=True)  146 us
    reduce_scatter x1, waiting for transfers between devices, per_device(): lax.psum_scatter(block_terms, 'mp', scatter_dimension=0, tiled=True)  47.3 us
    all_gather x1, waiting for transfers between devices, per_device(): pair_weights = lax.all_gather(both_weights, 'cc', axis=1, tiled=True)  22.5 us
    dot_general x1, matrix products, per_device(): jnp.dot(x_half, pair_weights, preferred_element_type=jnp.float32)  9.31 us
  transfers between devices with their start and end apart: 5, of which 4 were waited for; matrix products, arithmetic and copies ran while one was open for 6% of the time, Pallas kernels for 0%

profile of v2, /device:TPU:1, one launch (start us, length us, event | category | flops | bytes accessed | tf_op | source)
XLA Modules:
  0.0 425.7 jit_solution(6835526162539869750)
XLA Ops:
  7.2 2.3 pad_maximum_fusion
  9.6 0.7 all-gather.8.cloned.1.call-update
  10.3 0.6 compare_reduce_fusion.1
  11.0 0.6 compare_reduce_fusion
  11.6 1.3 fusion.32
  12.9 0.7 fusion.31
  14.0 1.4 pad_maximum_fusion.2
  15.4 22.5 %all-gather.6.cloned.1.call-done = bf16[1024,1024]{1,0:T(8,128)(2,1)} async-done(((bf16[1024,512]{1,0:T(8,128)(2,1)}), bf16[1024,1024]{1,0:T(8,128)(2,1)}) %all-gather.6.cloned.1.call-update) | async-done | bytes 2097168 | tf_op jit(solution)/shard_map/all_gather | solution.py:56
  37.9 157.3 %all-gather.8.cloned.1.call-done = bf16[2048,1024]{1,0:T(8,128)(2,1)} async-done(((bf16[64,1024]{1,0:T(8,128)(2,1)}), bf16[2048,1024]{1,0:T(8,128)(2,1)}) %all-gather.8.cloned.1.call-update) | async-done | bytes 4194320 | tf_op jit(solution)/shard_map/all_gather | solution.py:57
  195.2 9.3 %convert_bitcast_fusion = bf16[2048,1024]{0,1:T(8,128)(2,1)} fusion(bf16[1024,1024]{1,0:T(8,128)(2,1)} %all-gather.6.cloned.1.call-done, bf16[2048,1024]{1,0:T(8,128)(2,1)} %all-gather.8.cloned.1.call-done), kind=kOutput, calls=%fused_computation.8 | convolution fusion | flops 4297064448 | bytes 10485760 | tf_op jit(solution)/shard_map/dot_general | solution.py:58
  204.5 0.6 copy-done.3
  205.2 145.6 %all-gather.4.cloned.1.call-done = bf16[4096,384]{1,0:T(8,128)(2,1)} async-done(((bf16[64,384]{1,0:T(8,128)(2,1)}), bf16[4096,384]{1,0:T(8,128)(2,1)}) %all-gather.4.cloned.1.call-update) | async-done | bytes 3145744 | tf_op jit(solution)/shard_map/all_gather | solution.py:24
  350.8 1.5 slice_convert_fusion
  352.3 1.2 fusion.9
  353.5 0.2 broadcast_compare_fusion
  353.7 1.7 fusion
  355.4 3.2 copy-done.1
  358.6 2.4 fusion.3
  361.0 47.3 %reduce-scatter.2.cloned.1.call-done = bf16[256,1024]{0,1:T(8,128)(2,1)} async-done(((bf16[2048,1024]{0,1:T(8,128)(2,1)}), bf16[256,1024]{0,1:T(8,128)(2,1)}) %reduce-scatter.2.cloned.1.call-update) | async-done | bytes 524304 | tf_op jit(solution)/shard_map/reduce_scatter | solution.py:61
  408.3 1.1 convert_element_type.53
  409.7 2.6 collective-permute-start
  412.4 4.9 %fusion.16 = bf16[64,1,8,128]{3,0,2,1:T(8,128)(2,1)S(1)} fusion(f32[4096,64,8]{0,1,2:T(8,128)} %copy-done.1, f32[8,64]{1,0:T(8,128)S(1)} %broadcast_maximum_fusion, pred[64,4096]{1,0:T(8,128)(4,1)S(1)} %broadcast_compare_fusion, bf16[4096,384]{1,0:T(8,128)(2,1)S(1)} %copy-done.2, f32[8,64]{1,0:T(8,128)S(1)} %fusion.3), kind=kOutput, calls=%fused_computation.16 | convolution fusion | flops 545390592 | bytes 9838592 | tf_op jit(solution)/shard_map/gjts,sgd->gjtd/dot_general | solution.py:43
  417.4 0.7 copy.34
  418.4 0.7 copy.24
  (27 shorter events, 1.3 us)
Async XLA Ops:
  7.2 346.5 %copy-start = (bf16[64,1024]{1,0:T(8,128)(2,1)S(1)}, bf16[64,1024]{1,0:T(8,128)(2,1)}, u32[]{:S(2)}) copy-start(bf16[64,1024]{1,0:T(8,128)(2,1)} %param.11) | copy-start | bytes 393220
  7.2 30.7 %all-gather.6.cloned.1.call-start = ((), (), s32[]{:S(2)}) async-start(), calls=%async_computation.2 | async-start | bytes 3145728 | tf_op jit(solution)/shard_map/all_gather | solution.py:56
  9.5 185.7 %all-gather.8.cloned.1.call-start = ((), (), s32[]{:S(2)}) async-start(), calls=%async_computation.3 | async-start | bytes 4325376 | tf_op jit(solution)/shard_map/all_gather | solution.py:57
  10.3 340.5 %all-gather.4.cloned.1.call-start = ((), (), s32[]{:S(2)}) async-start(), calls=%async_computation.1 | async-start | bytes 3194880 | tf_op jit(solution)/shard_map/all_gather | solution.py:24
  15.4 392.9 %reduce-scatter.2.cloned.1.call-start = ((), (), s32[]{:S(2)}) async-start(), calls=%async_computation.4 | async-start | bytes 4718592 | tf_op jit(solution)/shard_map/reduce_scatter | solution.py:61
  204.5 0.7 copy-start.3
  350.8 2.9 copy-start.2
  355.4 3.2 copy-start.1
  409.7 8.3 %collective-permute-start = (bf16[256,256]{0,1:T(8,128)(2,1)S(1)}, bf16[256,256]{0,1:T(8,128)(2,1)S(1)}, u32[]{:S(2)}, u32[]{:S(2)}) collective-permute-start(bf16[256,256]{0,1:T(8,128)(2,1)S(1)} %get-tuple-element.32), channel_id=1, source_target_pairs={{0,8},{8,0},{1,9},{9,1},{2,10},{10,2},{3,11},{11,3},{4,12},{12,4},... | collective-permute-start | bytes 393224 | tf_op jit(solution)/shard_map/ppermute | solution.py:74
Sparse Core Ops, SparseCore 0:
  10.1 27.7 all-gather.5
  41.0 154.1 all-gather.7
  199.1 151.6 all-gather.3
  353.5 54.7 reduce-scatter.1

commit v3 on v1

--- a/solution.py
+++ b/solution.py
@@ -19,12 +19,14 @@
     pos_cols = jnp.zeros((tok_rows, HEAD), jnp.bfloat16)
     pos_cols = pos_cols.at[:, 0].set(pos_hi.astype(jnp.bfloat16))
     pos_cols = pos_cols.at[:, 1].set(pos_lo.astype(jnp.bfloat16))
-    kv_pack = jnp.concatenate((keys, values, pos_cols), axis=1)
-    kv_all = lax.all_gather(kv_pack, "ctx", axis=0, tiled=True)
+    x_width = x_normed.shape[1]
     kv_width = keys.shape[1]
-    k_piece = kv_all[:, :kv_width]
-    v_piece = kv_all[:, kv_width : 2 * kv_width]
-    pos_back = kv_all[:, 2 * kv_width :].astype(jnp.float32)
+    pack = jnp.concatenate((x_normed, keys, values, pos_cols), axis=1)
+    pack_all = lax.all_gather(pack, "ctx", axis=0, tiled=True)
+    x_all = pack_all[:, :x_width]
+    k_piece = pack_all[:, x_width : x_width + kv_width]
+    v_piece = pack_all[:, x_width + kv_width : x_width + 2 * kv_width]
+    pos_back = pack_all[:, x_width + 2 * kv_width :].astype(jnp.float32)
     k_pos = pos_back[:, 0] * 64.0 + pos_back[:, 1]
     q_pos = positions.astype(jnp.float32)
     count = k_piece.shape[0]
@@ -53,7 +55,7 @@
     hidden_cols = w_gate.shape[1]
     both_weights = jnp.concatenate((w_gate, w_up), axis=1)
     block_terms = jnp.dot(
-        lax.all_gather(x_normed, "ctx", axis=0, tiled=True),
+        x_all,
         both_weights,
         preferred_element_type=jnp.float32,
     ).astype(jnp.bfloat16)

time: 394 us -> 268 us (0.68)
  waiting for transfers between devices: 351 us -> 225 us
    all_gather x2 -> x1, waiting for transfers between devices: 304 us -> 181 us  [per_device(): pack_all = lax.all_gather(pack, 'ctx', axis=0, tiled=True)]
  transfers between devices with their start and end apart: 3 -> 2, of which waited for: 3 -> 2; matrix products, arithmetic and copies ran while one was open for 7% -> 4% of each run, Pallas kernels for 0% -> 0%
where the time goes in v3:
time: 268 us
  waiting for transfers between devices  225 us (84%)
  matrix products  15.8 us (6%)
  between operations  14.1 us (5%)
  other arithmetic  12 us (4%)
    all_gather x1, waiting for transfers between devices, per_device(): pack_all = lax.all_gather(pack, 'ctx', axis=0, tiled=True)  181 us
    reduce_scatter x1, waiting for transfers between devices, per_device(): lax.psum_scatter(block_terms.astype(jnp.float32).astype(jnp.bfloat16), 'm...  44 us
    dot_general x1, matrix products, per_device(): jnp.dot(x_all, both_weights, preferred_element_type=jnp.float32)  10.1 us
  transfers between devices with their start and end apart: 2, of which 2 were waited for; matrix products, arithmetic and copies ran while one was open for 4% of the time, Pallas kernels for 0%

profile of v3, /device:TPU:1, one launch (start us, length us, event | category | flops | bytes accessed | tf_op | source)
XLA Modules:
  0.0 267.8 jit_solution(8001370514653395683)
XLA Ops:
  7.2 0.0 all-gather.2.cloned.1.call-start
  7.2 0.6 compare_reduce_fusion
  7.9 0.6 compare_reduce_fusion.1
  8.5 1.3 fusion.32
  9.8 0.7 fusion.31
  10.5 0.1 copy.12
  10.6 0.1 copy.13
  10.7 0.1 scatter.9
  10.9 1.6 pad_maximum_fusion
  12.5 0.0 all-gather.2.cloned.1.call-update
  12.5 0.0 reduce-scatter.2.cloned.1.call-start
  12.6 180.6 %all-gather.2.cloned.1.call-done = bf16[4096,1408]{1,0:T(8,128)(2,1)} async-done(((bf16[64,1408]{1,0:T(8,128)(2,1)}), bf16[4096,1408]{1,0:T(8,128)(2,1)}) %all-gather.2.cloned.1.call-update) | async-done | bytes 11534352 | tf_op jit(solution)/shard_map/all_gather | solution.py:25
  193.2 10.1 %fusion.7 = bf16[4096,512]{1,0:T(8,128)(2,1)} fusion(bf16[4096,1408]{1,0:T(8,128)(2,1)} %all-gather.2.cloned.1.call-done, bf16[1024,256]{1,0:T(8,128)(2,1)} %param.17, bf16[1024,256]{1,0:T(8,128)(2,1)} %param.16), kind=kOutput, calls=%fused_computation.9 | convolution fusion | flops 4299161600 | bytes 13631488 | tf_op jit(solution)/shard_map/dot_general | solution.py:57
  203.4 1.4 slice_convert_fusion
  204.8 1.2 fusion.14
  205.9 0.2 broadcast_compare_fusion
  206.2 2.9 %fusion.2 = (f32[8,64]{1,0:T(8,128)S(1)}, f32[4096,64,8]{0,1,2:T(8,128)S(1)}) fusion(pred[64,4096]{1,0:T(8,128)(4,1)S(1)} %broadcast_compare_fusion, bf16[4096,1408]{1,0:T(8,128)(2,1)} %all-gather.2.cloned.1.call-done, bf16[64,1024]{1,0:T(8,128)(2,1)S(1)} %copy-done), kind=kOutput, calls=%fused_computation.4 | convolution fusion | flops 543161856 | bytes 9832448 | tf_op jit(solution)/shard_map/tgjd,sgd->gjts/dot_general | solution.py:36
  209.1 2.4 fusion.5
  211.5 2.8 %fusion.21 = bf16[64,1,8,128]{3,0,2,1:T(8,128)(2,1)S(1)} fusion(f32[4096,64,8]{0,1,2:T(8,128)S(1)} %get-tuple-element.29, f32[8,64]{1,0:T(8,128)S(1)} %broadcast_maximum_fusion, pred[64,4096]{1,0:T(8,128)(4,1)S(1)} %broadcast_compare_fusion, bf16[4096,1408]{1,0:T(8,128)(2,1)} %all-gather.2.cloned.1.call-done, f32[8,64]{1,0:T(8,128)S(1)} %fusion.5), kind=kOutput, calls=%fused_computation.18 | convolution fusion | flops 545390592 | bytes 9834496 | tf_op jit(solution)/shard_map/gjts,sgd->gjtd/dot_general | solution.py:44
  214.2 0.1 copy.15
  214.3 0.7 copy.25
  215.0 44.0 %reduce-scatter.2.cloned.1.call-done = bf16[512,512]{1,0:T(8,128)(2,1)} async-done(((bf16[4096,512]{1,0:T(8,128)(2,1)}), bf16[512,512]{1,0:T(8,128)(2,1)}) %reduce-scatter.2.cloned.1.call-update) | async-done | bytes 524304 | tf_op jit(solution)/shard_map/reduce_scatter | solution.py:62
  259.0 1.2 convert_element_type.48
  260.1 0.9 fusion.28
  (8 shorter events, 0.0 us)
Async XLA Ops:
  7.2 199.0 %copy-start = (bf16[64,1024]{1,0:T(8,128)(2,1)S(1)}, bf16[64,1024]{1,0:T(8,128)(2,1)}, u32[]{:S(2)}) copy-start(bf16[64,1024]{1,0:T(8,128)(2,1)} %param.11) | copy-start | bytes 393220
  7.2 186.0 %all-gather.2.cloned.1.call-start = ((), (), s32[]{:S(2)}) async-start(), calls=%async_computation.1 | async-start | bytes 11714560 | tf_op jit(solution)/shard_map/all_gather | solution.py:25
  12.5 190.9 %copy-start.1 = (s32[64]{0:T(128)S(1)}, s32[64]{0:T(128)}, u32[]{:S(2)}) copy-start(s32[64]{0:T(128)} %param.14) | copy-start | bytes 772
  12.5 246.4 %reduce-scatter.2.cloned.1.call-start = ((), (), s32[]{:S(2)}) async-start(), calls=%async_computation.2 | async-start | bytes 4718592 | tf_op jit(solution)/shard_map/reduce_scatter | solution.py:62
Sparse Core Ops, SparseCore 0:
  12.6 180.5 all-gather.1
  203.5 55.4 reduce-scatter.1

commit v4 on v3

--- a/solution.py
+++ b/solution.py
@@ -16,9 +16,10 @@
     top_run = jnp.full((local_kv, group, tok_rows), -1e30, jnp.float32)
     pos_hi = positions // 64
     pos_lo = positions - pos_hi * 64
-    pos_cols = jnp.zeros((tok_rows, HEAD), jnp.bfloat16)
-    pos_cols = pos_cols.at[:, 0].set(pos_hi.astype(jnp.bfloat16))
-    pos_cols = pos_cols.at[:, 1].set(pos_lo.astype(jnp.bfloat16))
+    col = lax.broadcasted_iota(jnp.int32, (tok_rows, HEAD), 1)
+    pos_cols = jnp.where(
+        col == 0, pos_hi[:, None], jnp.where(col == 1, pos_lo[:, None], 0)
+    ).astype(jnp.bfloat16)
     x_width = x_normed.shape[1]
     kv_width = keys.shape[1]
     pack = jnp.concatenate((x_normed, keys, values, pos_cols), axis=1)

time: 268 us -> 267 us (level)
    another operation x4 -> x0, other arithmetic: 3.24 us -> none
where the time goes in v4:
time: 267 us
  waiting for transfers between devices  227 us (85%)
  matrix products  15.8 us (6%)
  between operations  14.1 us (5%)
  other arithmetic  9.61 us (4%)
    all_gather x1, waiting for transfers between devices, per_device(): pack_all = lax.all_gather(pack, 'ctx', axis=0, tiled=True)  183 us
    reduce_scatter x1, waiting for transfers between devices, per_device(): lax.psum_scatter(block_terms.astype(jnp.float32).astype(jnp.bfloat16), 'm...  44 us
    dot_general x1, matrix products, per_device(): jnp.dot(x_all, both_weights, preferred_element_type=jnp.float32)  10.1 us
  transfers between devices with their start and end apart: 2, of which 2 were waited for; matrix products, arithmetic and copies ran while one was open for 4% of the time, Pallas kernels for 0%

profile of v4, /device:TPU:1, one launch (start us, length us, event | category | flops | bytes accessed | tf_op | source)
XLA Modules:
  0.0 267.0 jit_solution(17130365817435236402)
XLA Ops:
  7.2 0.0 copy-start
  7.2 0.0 all-gather.2.cloned.1.call-start
  7.2 0.7 multiply_subtract_fusion
  8.0 0.1 select_convert_fusion
  8.1 1.6 pad_maximum_fusion
  9.7 0.0 all-gather.2.cloned.1.call-update
  9.7 0.0 reduce-scatter.2.cloned.1.call-start
  9.8 182.7 %all-gather.2.cloned.1.call-done = bf16[4096,1408]{1,0:T(8,128)(2,1)} async-done(((bf16[64,1408]{1,0:T(8,128)(2,1)}), bf16[4096,1408]{1,0:T(8,128)(2,1)}) %all-gather.2.cloned.1.call-update) | async-done | bytes 11534352 | tf_op jit(solution)/shard_map/all_gather | solution.py:26
  192.4 10.1 %fusion.7 = bf16[4096,512]{1,0:T(8,128)(2,1)} fusion(bf16[4096,1408]{1,0:T(8,128)(2,1)} %all-gather.2.cloned.1.call-done, bf16[1024,256]{1,0:T(8,128)(2,1)} %param.13, bf16[1024,256]{1,0:T(8,128)(2,1)} %param.12), kind=kOutput, calls=%fused_computation.9 | convolution fusion | flops 4299161600 | bytes 13631488 | tf_op jit(solution)/shard_map/dot_general | solution.py:58
  202.6 0.0 reduce-scatter.2.cloned.1.call-update
  202.6 1.4 slice_convert_fusion
  204.0 1.2 fusion.14
  205.1 0.2 broadcast_compare_fusion
  205.4 0.0 copy-done
  205.4 2.9 %fusion.2 = (f32[8,64]{1,0:T(8,128)S(1)}, f32[4096,64,8]{0,1,2:T(8,128)S(1)}) fusion(pred[64,4096]{1,0:T(8,128)(4,1)S(1)} %broadcast_compare_fusion, bf16[4096,1408]{1,0:T(8,128)(2,1)} %all-gather.2.cloned.1.call-done, bf16[64,1024]{1,0:T(8,128)(2,1)S(1)} %copy-done), kind=kOutput, calls=%fused_computation.4 | convolution fusion | flops 543161856 | bytes 9832448 | tf_op jit(solution)/shard_map/tgjd,sgd->gjts/dot_general | solution.py:37
  208.3 2.4 fusion.5
  210.7 2.8 %fusion.21 = bf16[64,1,8,128]{3,0,2,1:T(8,128)(2,1)S(1)} fusion(f32[4096,64,8]{0,1,2:T(8,128)S(1)} %get-tuple-element.6, f32[8,64]{1,0:T(8,128)S(1)} %broadcast_maximum_fusion, pred[64,4096]{1,0:T(8,128)(4,1)S(1)} %broadcast_compare_fusion, bf16[4096,1408]{1,0:T(8,128)(2,1)} %all-gather.2.cloned.1.call-done, f32[8,64]{1,0:T(8,128)S(1)} %fusion.5), kind=kOutput, calls=%fused_computation.18 | convolution fusion | flops 545390592 | bytes 9834496 | tf_op jit(solution)/shard_map/gjts,sgd->gjtd/dot_general | solution.py:45
  213.4 0.1 copy.11
  213.5 0.7 copy.21
  214.2 44.0 %reduce-scatter.2.cloned.1.call-done = bf16[512,512]{1,0:T(8,128)(2,1)} async-done(((bf16[4096,512]{1,0:T(8,128)(2,1)}), bf16[512,512]{1,0:T(8,128)(2,1)}) %reduce-scatter.2.cloned.1.call-update) | async-done | bytes 524304 | tf_op jit(solution)/shard_map/reduce_scatter | solution.py:63
  258.2 1.2 convert_element_type.44
  259.3 0.9 fusion.28
  (2 shorter events, 0.0 us)
Async XLA Ops:
  7.2 198.2 %copy-start = (bf16[64,1024]{1,0:T(8,128)(2,1)S(1)}, bf16[64,1024]{1,0:T(8,128)(2,1)}, u32[]{:S(2)}) copy-start(bf16[64,1024]{1,0:T(8,128)(2,1)} %param.7) | copy-start | bytes 393220
  7.2 185.2 %all-gather.2.cloned.1.call-start = ((), (), s32[]{:S(2)}) async-start(), calls=%async_computation.1 | async-start | bytes 11714560 | tf_op jit(solution)/shard_map/all_gather | solution.py:26
  9.7 248.5 %reduce-scatter.2.cloned.1.call-start = ((), (), s32[]{:S(2)}) async-start(), calls=%async_computation.2 | async-start | bytes 4718592 | tf_op jit(solution)/shard_map/reduce_scatter | solution.py:63
Sparse Core Ops, SparseCore 0:
  11.8 180.5 all-gather.1
  202.7 55.4 reduce-scatter.1

commit v5 on v4

--- a/solution.py
+++ b/solution.py
@@ -60,9 +60,15 @@
         both_weights,
         preferred_element_type=jnp.float32,
     ).astype(jnp.bfloat16)
-    summed = lax.psum_scatter(
-        block_terms.astype(jnp.float32).astype(jnp.bfloat16), "mp", scatter_dimension=0, tiled=True
+    gate_sum = lax.psum_scatter(
+        block_terms[:, :hidden_cols], "mp", scatter_dimension=0, tiled=True
     ).astype(jnp.float32)
+    n_mp = lax.axis_size("mp")
+    up_parts = lax.all_to_all(
+        block_terms[:, hidden_cols:].reshape(n_mp, -1, hidden_cols), "mp", 0, 0, tiled=True
+    )
+    up_sum = up_parts.astype(jnp.float32).sum(axis=0)
+    summed = jnp.concatenate((gate_sum, up_sum), axis=1)
     gate = summed[:, :hidden_cols]
     up = summed[:, hidden_cols:]
     mlp_hidden = (jax.nn.silu(gate) * up).astype(jnp.bfloat16)

time: 267 us -> 270 us (1.011); the launches traced: 267 us -> 267 us
  waiting for transfers between devices: 227 us -> 222 us
  starting transfers between devices: 0.08 us -> 4.09 us
    reduce_scatter x1, waiting for transfers between devices: 44 us -> 19.2 us  [per_device(): lax.psum_scatter(block_terms[:, :hidden_cols], 'mp', scatter_dimension=0,...]
    all_to_all x0 -> x1, waiting for transfers between devices: none -> 19.5 us  [per_device(): lax.all_to_all(block_terms[:, hidden_cols:].reshape(n_mp, -1, hidden_cols...]
    all_to_all x0 -> x1, starting transfers between devices: none -> 4.01 us  [per_device(): lax.all_to_all(block_terms[:, hidden_cols:].reshape(n_mp, -1, hidden_cols...]
  transfers between devices with their start and end apart: 2 -> 3, of which waited for: 2 -> 3; matrix products, arithmetic and copies ran while one was open for 4% -> 4% of each run, Pallas kernels for 0% -> 0%
where the time goes in v5:
time: 270 us; the launch traced here: 267 us
  waiting for transfers between devices  222 us (82%)
  between operations  14.1 us (5%)
  matrix products  13.8 us (5%)
  other arithmetic  9.68 us (4%)
  starting transfers between devices  4.09 us (2%)
  local copies, waits for them, and re-layouts  3.09 us (1%)
    all_gather x1, waiting for transfers between devices, per_device(): pack_all = lax.all_gather(pack, 'ctx', axis=0, tiled=True)  183 us
    all_to_all x1, waiting for transfers between devices, per_device(): lax.all_to_all(block_terms[:, hidden_cols:].reshape(n_mp, -1, hidden_cols...  19.5 us
    reduce_scatter x1, waiting for transfers between devices, per_device(): lax.psum_scatter(block_terms[:, :hidden_cols], 'mp', scatter_dimension=0,...  19.2 us
    dot_general x1, matrix products, per_device(): jnp.dot(x_all, both_weights, preferred_element_type=jnp.float32)  8.1 us
  transfers between devices with their start and end apart: 3, of which 3 were waited for; matrix products, arithmetic and copies ran while one was open for 4% of the time, Pallas kernels for 0%

profile of v5, /device:TPU:1, one launch (start us, length us, event | category | flops | bytes accessed | tf_op | source)
XLA Modules:
  0.0 266.8 jit_solution(2301221563362550902)
XLA Ops:
  7.2 0.0 copy-start
  7.2 0.0 all-gather.2.cloned.1.call-start
  7.2 0.7 multiply_subtract_fusion
  8.0 0.1 select_convert_fusion
  8.1 1.6 pad_maximum_fusion
  9.7 0.0 all-gather.2.cloned.1.call-update
  9.7 182.7 %all-gather.2.cloned.1.call-done = bf16[4096,1408]{1,0:T(8,128)(2,1)} async-done(((bf16[64,1408]{1,0:T(8,128)(2,1)}), bf16[4096,1408]{1,0:T(8,128)(2,1)}) %all-gather.2.cloned.1.call-update) | async-done | bytes 11534352 | tf_op jit(solution)/shard_map/all_gather | solution.py:26
  192.4 8.1 %fusion.7 = bf16[4096,512]{1,0:T(8,128)(2,1)S(1)} fusion(bf16[4096,1408]{1,0:T(8,128)(2,1)} %all-gather.2.cloned.1.call-done, bf16[1024,256]{1,0:T(8,128)(2,1)} %param.13, bf16[1024,256]{1,0:T(8,128)(2,1)} %param.12), kind=kOutput, calls=%fused_computation.9 | convolution fusion | flops 4299161600 | bytes 13631488 | tf_op jit(solution)/shard_map/dot_general | solution.py:58
  200.5 2.3 fusion.38
  202.8 4.0 %all-to-all-start = ((bf16[8,512,256]{2,1,0:T(8,128)(2,1)}), bf16[8,512,256]{2,1,0:T(8,128)(2,1)S(1)}, u32[]{:S(2)}, u32[]{:S(2)}) async-start(bf16[8,512,256]{2,1,0:T(8,128)(2,1)} %bitcast.61), calls=%async_computation.1 | async-start | bytes 4194304 | tf_op jit(solution)/shard_map/all_to_all | solution.py:67
  206.9 0.0 reduce-scatter.2.cloned.1.call-start
  206.9 0.7 reduce-scatter.2.cloned.1.call-update
  207.6 1.4 slice_convert_fusion
  209.0 1.2 fusion.14
  210.2 0.2 broadcast_compare_fusion
  210.4 2.9 %fusion.2 = (f32[8,64]{1,0:T(8,128)S(1)}, f32[4096,64,8]{0,1,2:T(8,128)S(1)}) fusion(pred[64,4096]{1,0:T(8,128)(4,1)S(1)} %broadcast_compare_fusion, bf16[4096,1408]{1,0:T(8,128)(2,1)} %all-gather.2.cloned.1.call-done, bf16[64,1024]{1,0:T(8,128)(2,1)S(1)} %copy-done), kind=kOutput, calls=%fused_computation.4 | convolution fusion | flops 543161856 | bytes 9832448 | tf_op jit(solution)/shard_map/tgjd,sgd->gjts/dot_general | solution.py:37
  213.3 2.4 fusion.5
  215.7 2.8 %fusion.21 = bf16[64,1,8,128]{3,0,2,1:T(8,128)(2,1)S(1)} fusion(f32[4096,64,8]{0,1,2:T(8,128)S(1)} %get-tuple-element.8, f32[8,64]{1,0:T(8,128)S(1)} %broadcast_maximum_fusion, pred[64,4096]{1,0:T(8,128)(4,1)S(1)} %broadcast_compare_fusion, bf16[4096,1408]{1,0:T(8,128)(2,1)} %all-gather.2.cloned.1.call-done, f32[8,64]{1,0:T(8,128)S(1)} %fusion.5), kind=kOutput, calls=%fused_computation.19 | convolution fusion | flops 545390592 | bytes 9834496 | tf_op jit(solution)/shard_map/gjts,sgd->gjtd/dot_general | solution.py:45
  218.4 0.1 copy.11
  218.5 0.7 copy.21
  219.2 19.5 %all-to-all-done = bf16[8,512,256]{2,1,0:T(8,128)(2,1)S(1)} async-done(((bf16[8,512,256]{2,1,0:T(8,128)(2,1)}), bf16[8,512,256]{2,1,0:T(8,128)(2,1)S(1)}, u32[]{:S(2)}, u32[]{:S(2)}) %all-to-all-start) | async-done | bytes 2097184 | tf_op jit(solution)/shard_map/all_to_all | solution.py:67
  238.7 0.3 convert_reduce_fusion
  239.0 19.2 %reduce-scatter.2.cloned.1.call-done = bf16[512,256]{1,0:T(8,128)(2,1)} async-done(((bf16[4096,256]{1,0:T(8,128)(2,1)}), bf16[512,256]{1,0:T(8,128)(2,1)}) %reduce-scatter.2.cloned.1.call-update) | async-done | bytes 262160 | tf_op jit(solution)/shard_map/reduce_scatter | solution.py:63
  258.1 1.8 fusion.32
  (3 shorter events, 0.0 us)
Async XLA Ops:
  7.2 203.2 %copy-start = (bf16[64,1024]{1,0:T(8,128)(2,1)S(1)}, bf16[64,1024]{1,0:T(8,128)(2,1)}, u32[]{:S(2)}) copy-start(bf16[64,1024]{1,0:T(8,128)(2,1)} %param.7) | copy-start | bytes 393220
  7.2 185.2 %all-gather.2.cloned.1.call-start = ((), (), s32[]{:S(2)}) async-start(), calls=%async_computation.2 | async-start | bytes 11714560 | tf_op jit(solution)/shard_map/all_gather | solution.py:26
  202.8 35.8 %all-to-all-start = ((bf16[8,512,256]{2,1,0:T(8,128)(2,1)}), bf16[8,512,256]{2,1,0:T(8,128)(2,1)S(1)}, u32[]{:S(2)}, u32[]{:S(2)}) async-start(bf16[8,512,256]{2,1,0:T(8,128)(2,1)} %bitcast.61), calls=%async_computation.1 | async-start | bytes 4194304 | tf_op jit(solution)/shard_map/all_to_all | solution.py:67
  206.9 51.3 %reduce-scatter.2.cloned.1.call-start = ((), (), s32[]{:S(2)}) async-start(), calls=%async_computation.3 | async-start | bytes 2359296 | tf_op jit(solution)/shard_map/reduce_scatter | solution.py:63
Sparse Core Ops, SparseCore 0:
  11.8 180.5 all-gather.1
  210.5 47.5 reduce-scatter.1

commit v6 on v4

--- a/solution.py
+++ b/solution.py
@@ -60,9 +60,11 @@
         both_weights,
         preferred_element_type=jnp.float32,
     ).astype(jnp.bfloat16)
-    summed = lax.psum_scatter(
-        block_terms.astype(jnp.float32).astype(jnp.bfloat16), "mp", scatter_dimension=0, tiled=True
-    ).astype(jnp.float32)
+    n_mp = lax.axis_size("mp")
+    parts = lax.all_to_all(
+        block_terms.reshape(n_mp, -1, 2 * hidden_cols), "mp", 0, 0, tiled=True
+    )
+    summed = parts.astype(jnp.float32).sum(axis=0)
     gate = summed[:, :hidden_cols]
     up = summed[:, hidden_cols:]
     mlp_hidden = (jax.nn.silu(gate) * up).astype(jnp.bfloat16)

time: 267 us -> 267 us (level)
  waiting for transfers between devices: 227 us -> 220 us
  starting transfers between devices: 0.08 us -> 4.59 us
    reduce_scatter x1 -> x0, waiting for transfers between devices: 44 us -> none  [per_device(): lax.psum_scatter(block_terms.astype(jnp.float32).astype(jnp.bfloat16), 'm...]
    all_to_all x0 -> x1, waiting for transfers between devices: none -> 37.1 us  [per_device(): lax.all_to_all(block_terms.reshape(n_mp, -1, 2 * hidden_cols), 'mp', 0, 0...]
    all_to_all x0 -> x1, starting transfers between devices: none -> 4.55 us  [per_device(): lax.all_to_all(block_terms.reshape(n_mp, -1, 2 * hidden_cols), 'mp', 0, 0...]
    reduce_sum x0 -> x1, other arithmetic: none -> 2.88 us  [per_device(): summed = parts.astype(jnp.float32).sum(axis=0)]
where the time goes in v6:
time: 267 us; the launch traced here: 266 us
  waiting for transfers between devices  220 us (82%)
  matrix products  15.7 us (6%)
  between operations  14.1 us (5%)
  other arithmetic  11.3 us (4%)
  starting transfers between devices  4.59 us (2%)
    all_gather x1, waiting for transfers between devices, per_device(): pack_all = lax.all_gather(pack, 'ctx', axis=0, tiled=True)  183 us
    all_to_all x1, waiting for transfers between devices, per_device(): lax.all_to_all(block_terms.reshape(n_mp, -1, 2 * hidden_cols), 'mp', 0, 0...  37.1 us
    dot_general x1, matrix products, per_device(): jnp.dot(x_all, both_weights, preferred_element_type=jnp.float32)  10.1 us
  transfers between devices with their start and end apart: 2, of which 2 were waited for; matrix products, arithmetic and copies ran while one was open for 4% of the time, Pallas kernels for 0%

profile of v6, /device:TPU:1, one launch (start us, length us, event | category | flops | bytes accessed | tf_op | source)
XLA Modules:
  0.0 266.3 jit_solution(10428760250981406191)
XLA Ops:
  7.2 0.0 copy-start
  7.2 0.0 all-gather.2.cloned.1.call-start
  7.2 0.7 multiply_subtract_fusion
  8.0 0.1 select_convert_fusion
  8.1 1.6 pad_maximum_fusion
  9.7 0.0 all-gather.2.cloned.1.call-update
  9.7 182.7 %all-gather.2.cloned.1.call-done = bf16[4096,1408]{1,0:T(8,128)(2,1)} async-done(((bf16[64,1408]{1,0:T(8,128)(2,1)}), bf16[4096,1408]{1,0:T(8,128)(2,1)}) %all-gather.2.cloned.1.call-update) | async-done | bytes 11534352 | tf_op jit(solution)/shard_map/all_gather | solution.py:26
  192.4 10.1 %fusion.7 = bf16[4096,512]{1,0:T(8,128)(2,1)} fusion(bf16[4096,1408]{1,0:T(8,128)(2,1)} %all-gather.2.cloned.1.call-done, bf16[1024,256]{1,0:T(8,128)(2,1)} %param.13, bf16[1024,256]{1,0:T(8,128)(2,1)} %param.12), kind=kOutput, calls=%fused_computation.10 | convolution fusion | flops 4299161600 | bytes 13631488 | tf_op jit(solution)/shard_map/dot_general | solution.py:58
  202.5 4.5 %all-to-all-start = ((bf16[8,512,512]{2,1,0:T(8,128)(2,1)}), bf16[8,512,512]{2,1,0:T(8,128)(2,1)}, u32[]{:S(2)}, u32[]{:S(2)}) async-start(bf16[8,512,512]{2,1,0:T(8,128)(2,1)} %bitcast.61), calls=%async_computation | async-start | bytes 8388608 | tf_op jit(solution)/shard_map/all_to_all | solution.py:64
  207.1 1.4 slice_convert_fusion
  208.4 1.2 fusion.14
  209.6 0.2 broadcast_compare_fusion
  209.8 0.0 copy-done
  209.8 2.9 %fusion.2 = (f32[8,64]{1,0:T(8,128)S(1)}, f32[4096,64,8]{0,1,2:T(8,128)S(1)}) fusion(pred[64,4096]{1,0:T(8,128)(4,1)S(1)} %broadcast_compare_fusion, bf16[4096,1408]{1,0:T(8,128)(2,1)} %all-gather.2.cloned.1.call-done, bf16[64,1024]{1,0:T(8,128)(2,1)S(1)} %copy-done), kind=kOutput, calls=%fused_computation.4 | convolution fusion | flops 543161856 | bytes 9832448 | tf_op jit(solution)/shard_map/tgjd,sgd->gjts/dot_general | solution.py:37
  212.7 2.4 fusion.5
  215.1 2.8 %fusion.21 = bf16[64,1,8,128]{3,0,2,1:T(8,128)(2,1)S(1)} fusion(f32[4096,64,8]{0,1,2:T(8,128)S(1)} %get-tuple-element.6, f32[8,64]{1,0:T(8,128)S(1)} %broadcast_maximum_fusion, pred[64,4096]{1,0:T(8,128)(4,1)S(1)} %broadcast_compare_fusion, bf16[4096,1408]{1,0:T(8,128)(2,1)} %all-gather.2.cloned.1.call-done, f32[8,64]{1,0:T(8,128)S(1)} %fusion.5), kind=kOutput, calls=%fused_computation.19 | convolution fusion | flops 545390592 | bytes 9834496 | tf_op jit(solution)/shard_map/gjts,sgd->gjtd/dot_general | solution.py:45
  217.9 0.1 copy.11
  218.0 0.7 copy.21
  218.7 37.1 %all-to-all-done = bf16[8,512,512]{2,1,0:T(8,128)(2,1)} async-done(((bf16[8,512,512]{2,1,0:T(8,128)(2,1)}), bf16[8,512,512]{2,1,0:T(8,128)(2,1)}, u32[]{:S(2)}, u32[]{:S(2)}) %all-to-all-start) | async-done | bytes 4194336 | tf_op jit(solution)/shard_map/all_to_all | solution.py:64
  255.7 2.9 %convert_reduce_fusion = f32[512,512]{1,0:T(8,128)S(1)} fusion(bf16[8,512,512]{2,1,0:T(8,128)(2,1)} %all-to-all-done), kind=kLoop, calls=%fused_computation.7 | loop fusion | flops 3932160 | bytes 5242880 | tf_op jit(solution)/shard_map/reduce_sum | solution.py:67
  258.6 0.9 fusion.28
  (2 shorter events, 0.0 us)
Async XLA Ops:
  7.2 202.7 %copy-start = (bf16[64,1024]{1,0:T(8,128)(2,1)S(1)}, bf16[64,1024]{1,0:T(8,128)(2,1)}, u32[]{:S(2)}) copy-start(bf16[64,1024]{1,0:T(8,128)(2,1)} %param.7) | copy-start | bytes 393220
  7.2 185.2 %all-gather.2.cloned.1.call-start = ((), (), s32[]{:S(2)}) async-start(), calls=%async_computation.1 | async-start | bytes 11714560 | tf_op jit(solution)/shard_map/all_gather | solution.py:26
  202.5 53.2 %all-to-all-start = ((bf16[8,512,512]{2,1,0:T(8,128)(2,1)}), bf16[8,512,512]{2,1,0:T(8,128)(2,1)}, u32[]{:S(2)}, u32[]{:S(2)}) async-start(bf16[8,512,512]{2,1,0:T(8,128)(2,1)} %bitcast.61), calls=%async_computation | async-start | bytes 8388608 | tf_op jit(solution)/shard_map/all_to_all | solution.py:64
Sparse Core Ops, SparseCore 0:
  11.8 180.5 all-gather.1

commit v7 on v6

--- a/solution.py
+++ b/solution.py
@@ -64,7 +64,9 @@
     parts = lax.all_to_all(
         block_terms.reshape(n_mp, -1, 2 * hidden_cols), "mp", 0, 0, tiled=True
     )
-    summed = parts.astype(jnp.float32).sum(axis=0)
+    summed = parts[0].astype(jnp.float32)
+    for index in range(1, n_mp):
+        summed = summed + parts[index].astype(jnp.float32)
     gate = summed[:, :hidden_cols]
     up = summed[:, hidden_cols:]
     mlp_hidden = (jax.nn.silu(gate) * up).astype(jnp.bfloat16)

time: 267 us -> 267 us (level)
    reduce_sum x1 -> x0, other arithmetic: 2.88 us -> none  [per_device(): summed = parts.astype(jnp.float32).sum(axis=0)]
    add x0 -> x1, other arithmetic: none -> 2.67 us  [per_device(): summed = summed + parts[index].astype(jnp.float32)]
where the time goes in v7:
time: 267 us; the launch traced here: 266 us
  waiting for transfers between devices  220 us (82%)
  matrix products  15.8 us (6%)
  between operations  14.1 us (5%)
  other arithmetic  11.1 us (4%)
  starting transfers between devices  4.58 us (2%)
    all_gather x1, waiting for transfers between devices, per_device(): pack_all = lax.all_gather(pack, 'ctx', axis=0, tiled=True)  183 us
    all_to_all x1, waiting for transfers between devices, per_device(): lax.all_to_all(block_terms.reshape(n_mp, -1, 2 * hidden_cols), 'mp', 0, 0...  37.1 us
    dot_general x1, matrix products, per_device(): jnp.dot(x_all, both_weights, preferred_element_type=jnp.float32)  10.1 us
  transfers between devices with their start and end apart: 2, of which 2 were waited for; matrix products, arithmetic and copies ran while one was open for 4% of the time, Pallas kernels for 0%

profile of v7, /device:TPU:1, one launch (start us, length us, event | category | flops | bytes accessed | tf_op | source)
XLA Modules:
  0.0 266.3 jit_solution(4063482619255102290)
XLA Ops:
  7.2 0.0 copy-start
  7.2 0.0 all-gather.2.cloned.1.call-start
  7.2 0.7 multiply_subtract_fusion
  8.0 0.1 select_convert_fusion
  8.1 1.6 pad_maximum_fusion
  9.7 0.0 all-gather.2.cloned.1.call-update
  9.7 182.9 %all-gather.2.cloned.1.call-done = bf16[4096,1408]{1,0:T(8,128)(2,1)} async-done(((bf16[64,1408]{1,0:T(8,128)(2,1)}), bf16[4096,1408]{1,0:T(8,128)(2,1)}) %all-gather.2.cloned.1.call-update) | async-done | bytes 11534352 | tf_op jit(solution)/shard_map/all_gather | solution.py:26
  192.6 10.1 %fusion.7 = bf16[4096,512]{1,0:T(8,128)(2,1)} fusion(bf16[4096,1408]{1,0:T(8,128)(2,1)} %all-gather.2.cloned.1.call-done, bf16[1024,256]{1,0:T(8,128)(2,1)} %param.13, bf16[1024,256]{1,0:T(8,128)(2,1)} %param.12), kind=kOutput, calls=%fused_computation.9 | convolution fusion | flops 4299161600 | bytes 13631488 | tf_op jit(solution)/shard_map/dot_general | solution.py:58
  202.7 4.5 %all-to-all-start = ((bf16[8,512,512]{2,1,0:T(8,128)(2,1)}), bf16[8,512,512]{2,1,0:T(8,128)(2,1)}, u32[]{:S(2)}, u32[]{:S(2)}) async-start(bf16[8,512,512]{2,1,0:T(8,128)(2,1)} %bitcast.63), calls=%async_computation | async-start | bytes 8388608 | tf_op jit(solution)/shard_map/all_to_all | solution.py:64
  207.3 1.4 slice_convert_fusion
  208.6 1.2 fusion.14
  209.8 0.2 broadcast_compare_fusion
  210.0 0.0 copy-done
  210.0 2.9 %fusion.2 = (f32[8,64]{1,0:T(8,128)S(1)}, f32[4096,64,8]{0,1,2:T(8,128)S(1)}) fusion(pred[64,4096]{1,0:T(8,128)(4,1)S(1)} %broadcast_compare_fusion, bf16[4096,1408]{1,0:T(8,128)(2,1)} %all-gather.2.cloned.1.call-done, bf16[64,1024]{1,0:T(8,128)(2,1)S(1)} %copy-done), kind=kOutput, calls=%fused_computation.4 | convolution fusion | flops 543161856 | bytes 9832448 | tf_op jit(solution)/shard_map/tgjd,sgd->gjts/dot_general | solution.py:37
  212.9 2.4 fusion.5
  215.3 2.8 %fusion.21 = bf16[64,1,8,128]{3,0,2,1:T(8,128)(2,1)S(1)} fusion(f32[4096,64,8]{0,1,2:T(8,128)S(1)} %get-tuple-element.6, f32[8,64]{1,0:T(8,128)S(1)} %broadcast_maximum_fusion, pred[64,4096]{1,0:T(8,128)(4,1)S(1)} %broadcast_compare_fusion, bf16[4096,1408]{1,0:T(8,128)(2,1)} %all-gather.2.cloned.1.call-done, f32[8,64]{1,0:T(8,128)S(1)} %fusion.5), kind=kOutput, calls=%fused_computation.18 | convolution fusion | flops 545390592 | bytes 9834496 | tf_op jit(solution)/shard_map/gjts,sgd->gjtd/dot_general | solution.py:45
  218.1 0.1 copy.11
  218.2 0.7 copy.21
  218.9 37.1 %all-to-all-done = bf16[8,512,512]{2,1,0:T(8,128)(2,1)} async-done(((bf16[8,512,512]{2,1,0:T(8,128)(2,1)}), bf16[8,512,512]{2,1,0:T(8,128)(2,1)}, u32[]{:S(2)}, u32[]{:S(2)}) %all-to-all-start) | async-done | bytes 4194336 | tf_op jit(solution)/shard_map/all_to_all | solution.py:64
  255.9 2.7 %add_bitcast_fusion = f32[512,512]{1,0:T(8,128)S(1)} fusion(bf16[8,512,512]{2,1,0:T(8,128)(2,1)} %all-to-all-done), kind=kLoop, calls=%fused_computation.26 | loop fusion | flops 3932160 | bytes 5242880 | tf_op jit(solution)/shard_map/add | solution.py:69
  258.6 0.9 fusion.28
  (2 shorter events, 0.0 us)
Async XLA Ops:
  7.2 202.9 %copy-start = (bf16[64,1024]{1,0:T(8,128)(2,1)S(1)}, bf16[64,1024]{1,0:T(8,128)(2,1)}, u32[]{:S(2)}) copy-start(bf16[64,1024]{1,0:T(8,128)(2,1)} %param.7) | copy-start | bytes 393220
  7.2 185.4 %all-gather.2.cloned.1.call-start = ((), (), s32[]{:S(2)}) async-start(), calls=%async_computation.1 | async-start | bytes 11714560 | tf_op jit(solution)/shard_map/all_gather | solution.py:26
  202.7 53.2 %all-to-all-start = ((bf16[8,512,512]{2,1,0:T(8,128)(2,1)}), bf16[8,512,512]{2,1,0:T(8,128)(2,1)}, u32[]{:S(2)}, u32[]{:S(2)}) async-start(bf16[8,512,512]{2,1,0:T(8,128)(2,1)} %bitcast.63), calls=%async_computation | async-start | bytes 8388608 | tf_op jit(solution)/shard_map/all_to_all | solution.py:64
Sparse Core Ops, SparseCore 0:
  11.8 180.7 all-gather.1
